TPU v7x, 256 devices: a whole 4x4x8 slice. The times are simulated.
256 devices in a mesh: pair: 16 (over z, core), virt: 16 (over x, y).
Axes of the slice: x: 4, y: 4, z: 8, core: 2. Of those that a mesh axis runs over, the one named last changes fastest.
Arguments:
- amplitudes: float32 [64, 2048, 4096], P('virt', 'pair'), may hold values from -0.9 to 0.9
- integrals: float32 [64, 384, 4096], P('virt', 'pair'), may hold values from -0.09375 to 0.09375
- tile_flags: int32 [64], P('virt'), may hold values 0 or 1
- live_count: int32 [16], replicated, may hold values from 1 to 4, as said below
- pair_occ: int32 [2048, 2], P(('pair', 'virt')), may hold values from 0 to 199
- occ_energy: float32 [200], replicated, may hold values from -2.5 to -0.3
- ab_energy: float32 [384], replicated, may hold values from 0.6 to 3
Outputs:
- ladder: float32 [2048, 384], P(('pair', 'virt'))
- update: float32 [2048, 384], P(('pair', 'virt'))
Inputs may be any that keep to these rules, and one draw needn't show every extreme that they name: `live_count`: entry v is how many of the 4 slots of virt index v hold tile pairs: its slots below that number do, and the contents of the others are not to be used. At some index it is 4, and at the index half the axis away it is 1.
All inputs are finite; a program needn't handle non-finite values. No bound on the sum of `tile_flags` on one device may be relied on, other than what follows from the above.
Results may differ from a plain program's by a relative error of at most 0.0001.
Values sent between devices are 32-bit elements; how exact they have to be, the bound alone decides.
No kernel may reach another device: no remote copies, remote signals or barrier semaphores. Data moves between devices by JAX's collectives and lax.ppermute only.
A program may use at most 128 MiB of HBM per device.

v0:
```python
import jax
import jax.numpy as jnp
from jax import lax
from jax.sharding import PartitionSpec as P

TILE = 64


def swap_in_tile(rows):
    shaped = rows.reshape(rows.shape[0], TILE, TILE)
    return jnp.swapaxes(shaped, 1, 2).reshape(rows.shape)


def symmetric_amps(amp_rows, flag):
    return amp_rows + flag.astype(jnp.float32) * swap_in_tile(amp_rows)


def tile_product(amp_tile, int_rows, precision=lax.Precision.HIGH):
    return lax.dot_general(
        amp_tile,
        int_rows,
        (((1,), (1,)), ((), ())),
        precision=precision,
        preferred_element_type=jnp.float32,
    )


def on_device(amplitudes, integrals, tile_flags, live_count, pair_occ, occ_energy, ab_energy):
    slots, pair_rows, _ = amplitudes.shape
    n_virt = lax.axis_size("virt")
    half = n_virt // 2
    virt_index = lax.axis_index("virt")
    partner = (virt_index + half) % n_virt
    columns = jnp.arange(n_virt, dtype=jnp.int32)
    neighbour = columns ^ 1
    across = jnp.roll(live_count, half)
    give_one = jnp.clip((live_count - across) // 2, 0, 1)
    take_one = jnp.clip((across - live_count) // 2, 0, 1)
    keep_one = live_count - give_one
    give_two = ((keep_one == 4) & (take_one[neighbour] == 0) & (keep_one[neighbour] <= 2)).astype(
        jnp.int32
    )
    take_two = give_two[neighbour]
    keep_all = keep_one - give_two
    own_count = live_count[virt_index]
    take = take_one[virt_index]
    take_y = take_two[virt_index]
    keep = keep_all[virt_index]
    send_at = own_count - 1
    send_amp = symmetric_amps(
        lax.dynamic_index_in_dim(amplitudes, send_at, 0, keepdims=False),
        lax.dynamic_index_in_dim(tile_flags, send_at, 0, keepdims=False),
    )
    send_int = lax.dynamic_index_in_dim(integrals, send_at, 0, keepdims=False)
    perm = [(v, (v + half) % n_virt) for v in range(n_virt)]
    recv_int = lax.ppermute(send_int, "virt", perm)
    recv_amp = lax.ppermute(send_amp, "virt", perm)
    perm_y = [(v, v ^ 1) for v in range(n_virt)]
    recv_int_y = lax.ppermute(integrals[3], "virt", perm_y)
    recv_amp_y = lax.ppermute(symmetric_amps(amplitudes[3], tile_flags[3]), "virt", perm_y)

    def own_amps(slot):
        return symmetric_amps(amplitudes[slot], tile_flags[slot])

    first_two = lax.all_gather(integrals[0:2], "pair", axis=1, tiled=True)
    running = tile_product(own_amps(0), first_two[0], lax.Precision.HIGHEST)
    second = tile_product(own_amps(1), first_two[1], lax.Precision.HIGHEST)
    running = running + jnp.where(keep > 1, second, jnp.zeros_like(second))
    third_int = jnp.where(take > 0, recv_int, jnp.where(take_y > 0, recv_int_y, integrals[2]))
    third_amp = jnp.where(take > 0, recv_amp, jnp.where(take_y > 0, recv_amp_y, own_amps(2)))
    third = tile_product(third_amp, lax.all_gather(third_int, "pair", axis=0, tiled=True))
    third_live = (take > 0) | (take_y > 0) | (keep > 2)
    running = running + jnp.where(third_live, third, jnp.zeros_like(third))

    def fourth(acc):
        gathered = lax.all_gather(integrals[3], "pair", axis=0, tiled=True)
        term = tile_product(own_amps(3), gathered)
        return acc + jnp.where(keep > 3, term, jnp.zeros_like(term))

    any_full = jnp.max(keep_all) > 3
    running = lax.cond(any_full, fourth, lambda acc: acc, running)
    ab = running.shape[1]
    blocks = running.reshape(n_virt, pair_rows // n_virt, ab)
    received = lax.all_to_all(blocks, "virt", 0, 0, tiled=False)
    ladder = jnp.sum(received, axis=0)
    occ_range = jnp.arange(occ_energy.shape[0], dtype=jnp.int32)
    first_energy = jnp.sum(
        jnp.where(pair_occ[:, 0:1] == occ_range[None, :], occ_energy[None, :], 0.0), axis=1
    )
    second_energy = jnp.sum(
        jnp.where(pair_occ[:, 1:2] == occ_range[None, :], occ_energy[None, :], 0.0), axis=1
    )
    denominator = ab_energy[None, :] - first_energy[:, None] - second_energy[:, None]
    return (ladder, ladder / denominator)


def solution(mesh):
    return jax.shard_map(
        on_device,
        mesh=mesh,
        in_specs=(
            P("virt", "pair", None),
            P("virt", "pair", None),
            P("virt"),
            P(),
            P(("pair", "virt"), None),
            P(),
            P(),
        ),
        out_specs=(P(("pair", "virt"), None), P(("pair", "virt"), None)),
        check_vma=False,
    )
```

profile of v0, /device:TPU:1, one launch (start us, length us, event | category | flops | bytes accessed | tf_op | source)
XLA Modules:
  0.0 164.5 jit_solution(631864503196057487)
XLA Ops:
  7.2 2.2 %slice.66 = f32[2,24,4096]{2,1,0:T(8,128)} slice(f32[4,24,4096]{2,1,0:T(8,128)} %param.10), slice={[0:2], [0:24], [0:4096]} | slice | bytes 1572864 | tf_op jit(solution)/shard_map/slice | solution.py:65
  11.5 3.6 %collective-permute-start.2 = (f32[24,4096]{1,0:T(8,128)S(1)}, f32[24,4096]{1,0:T(8,128)S(1)}, u32[]{:S(2)}, u32[]{:S(2)}) collective-permute-start(f32[24,4096]{1,0:T(8,128)S(1)} %get-tuple-element.42), channel_id=1, source_target_pairs={{0,8},{1,9},{2,10},{3,11},{4,12},{5,13},{6,14},{7,15},{8,0},{9,1},... | collective-permute-start | bytes 1179656 | tf_op jit(solution)/shard_map/ppermute | solution.py:56
  22.9 1.9 %collective-permute-done.3 = f32[24,4096]{1,0:T(8,128)S(1)} collective-permute-done((f32[24,4096]{1,0:T(8,128)S(1)}, f32[24,4096]{1,0:T(8,128)S(1)}, u32[]{:S(2)}, u32[]{:S(2)}) %collective-permute-start.3) | collective-permute-done | bytes 393248 | tf_op jit(solution)/shard_map/ppermute | solution.py:59
  25.7 8.3 %fusion.25 = (f32[1,128,4096]{2,1,0:T(8,128)}, f32[1,128,4096]{2,1,0:T(8,128)}, f32[1,128,4096]{2,1,0:T(8,128)}, f32[1,128,4096]{2,1,0:T(8,128)}, f32[1,128,4096]{2,1,0:T(8,128)}) fusion(f32[4,128,4096]{2,1,0:T(8,128)} %param.9, s32[]{:T(128)S(6)} %select_n.101), kind=kLoop, calls=%fused_computation.59 | loop fusion | bytes 20971524 | tf_op jit(solution)/shard_map/slice | solution.py:63
  34.0 1.9 %copy.41 = f32[1,128,4096]{1,2,0:T(8,128)S(1)} copy(f32[1,128,4096]{2,1,0:T(8,128)} %get-tuple-element.38) | data formatting | bytes 4194304
  40.3 2.1 %collective-permute-start = (f32[128,4096]{0,1:T(8,128)}, f32[128,4096]{0,1:T(8,128)}, u32[]{:S(2)}, u32[]{:S(2)}) collective-permute-start(f32[128,4096]{0,1:T(8,128)} %bitcast_add_fusion.3), channel_id=1, source_target_pairs={{0,8},{1,9},{2,10},{3,11},{4,12},{5,13},{6,14},{7,15},{8,0},{9,1},... | collective-permute-start | bytes 6291464 | tf_op jit(solution)/shard_map/ppermute | solution.py:57
  42.4 1.9 %copy.42 = f32[1,128,4096]{1,2,0:T(8,128)S(1)} copy(f32[1,128,4096]{2,1,0:T(8,128)} %get-tuple-element.37) | data formatting | bytes 4194304
  49.1 1.9 %copy.43 = f32[1,128,4096]{1,2,0:T(8,128)S(1)} copy(f32[1,128,4096]{2,1,0:T(8,128)} %get-tuple-element.36) | data formatting | bytes 4194304
  52.3 2.5 %copy.37 = f32[128,64,64]{0,2,1:T(8,128)} copy(f32[128,64,64]{0,1,2:T(8,128)S(1)} %bitcast.100) | data formatting | bytes 4194304 | tf_op jit(solution)/shard_map/mul | solution.py:15
  54.8 1.9 %copy.40 = f32[1,128,4096]{1,2,0:T(8,128)S(1)} copy(f32[1,128,4096]{2,1,0:T(8,128)} %get-tuple-element.39) | data formatting | bytes 4194304
  57.6 2.6 %copy.31 = f32[128,64,64]{0,2,1:T(8,128)} copy(f32[128,64,64]{0,1,2:T(8,128)S(1)} %bitcast.101) | data formatting | bytes 4194304 | tf_op jit(solution)/shard_map/mul | solution.py:15
  60.7 2.9 %copy.39 = f32[1,128,4096]{1,2,0:T(8,128)} copy(f32[1,128,4096]{2,1,0:T(8,128)} %get-tuple-element.40) | data formatting | bytes 4194304
  64.2 1.8 %broadcast_multiply_fusion.4 = f32[1,128,4096]{1,2,0:T(8,128)S(1)} fusion(f32[1,128,4096]{1,2,0:T(8,128)} %copy.39, f32[]{:T(128)} %bitcast.7), kind=kLoop, calls=%fused_computation.30 | loop fusion | flops 524288 | bytes 4194308 | tf_op jit(solution)/shard_map/mul | solution.py:15
  66.0 2.5 %copy.29 = f32[128,64,64]{0,2,1:T(8,128)} copy(f32[128,64,64]{0,1,2:T(8,128)S(1)} %bitcast.102) | data formatting | bytes 4194304 | tf_op jit(solution)/shard_map/mul | solution.py:15
  70.5 3.4 %bitcast_add_fusion.4 = f32[1,128,4096]{1,2,0:T(8,128)} fusion(f32[1,128,4096]{1,2,0:T(8,128)S(1)} %copy.40, f32[128,64,64]{0,2,1:T(8,128)} %copy.31), kind=kLoop, calls=%fused_computation.19 | loop fusion | flops 524288 | bytes 6291456 | tf_op jit(solution)/shard_map/add | solution.py:15
  75.5 11.9 %collective-permute-done = f32[128,4096]{0,1:T(8,128)} collective-permute-done((f32[128,4096]{0,1:T(8,128)}, f32[128,4096]{0,1:T(8,128)}, u32[]{:S(2)}, u32[]{:S(2)}) %collective-permute-start) | collective-permute-done | bytes 2097184 | tf_op jit(solution)/shard_map/ppermute | solution.py:57
  87.4 6.4 %collective-permute-done.1 = f32[128,4096]{0,1:T(8,128)} collective-permute-done((f32[128,4096]{0,1:T(8,128)}, f32[128,4096]{0,1:T(8,128)}, u32[]{:S(2)}, u32[]{:S(2)}) %collective-permute-start.1) | collective-permute-done | bytes 2097184 | tf_op jit(solution)/shard_map/ppermute | solution.py:60
  93.8 2.3 %fusion.11 = f32[128,4096]{0,1:T(8,128)} fusion(f32[128,4096]{0,1:T(8,128)} %collective-permute-done, f32[128,4096]{0,1:T(8,128)} %collective-permute-done.1, f32[128,64,64]{0,2,1:T(8,128)S(1)} %copy-done.7, f32[1,128,4096]{1,2,0:T(8,128)S(1)} %copy-done.2, pred[]{:T(512)} %bitcast.21, pred[]{:T(512)} %bitcast.20), kind=kLoop, calls=%fused_computation.15 | loop fusion | flops 1572864 | bytes 10485762 | tf_op jit(solution)/shard_map/jit(_where)/select_n | solution.py:70
  96.1 9.5 %fusion.17 = f32[128,384]{1,0:T(8,128)S(1)} fusion(f32[2,384,4096]{2,1,0:T(8,128)} %all-gather.7.cloned.1.call-done, f32[1,128,4096]{1,2,0:T(8,128)S(1)} %copy-done.4, pred[]{:T(512)S(6)} %gt.29), kind=kOutput, calls=%fused_computation.23 | convolution fusion | flops 2415968256 | bytes 8585217 | tf_op jit(solution)/shard_map/dot_general | solution.py:19
  105.7 9.8 %fusion.14 = f32[128,384]{1,0:T(8,128)S(1)} fusion(f32[128,384]{1,0:T(8,128)S(1)} %fusion.17, f32[2,384,4096]{2,1,0:T(8,128)} %all-gather.7.cloned.1.call-done, f32[1,128,4096]{1,2,0:T(8,128)S(1)} %copy-done.5), kind=kOutput, calls=%fused_computation.22 | convolution fusion | flops 2415968256 | bytes 8781824 | tf_op jit(solution)/shard_map/dot_general | solution.py:19
  115.5 20.6 %all-gather.9.cloned.1.call-done = f32[384,4096]{1,0:T(8,128)} async-done(((f32[24,4096]{1,0:T(8,128)}), f32[384,4096]{1,0:T(8,128)}) %all-gather.9.cloned.1.call-update) | async-done | bytes 6291472 | tf_op jit(solution)/shard_map/all_gather | solution.py:71
  136.1 7.1 %fusion.20 = f32[128,384]{1,0:T(8,128)} fusion(f32[128,384]{1,0:T(8,128)S(1)} %fusion.14, f32[128,4096]{0,1:T(8,128)S(1)} %copy-done.6, f32[384,4096]{1,0:T(8,128)} %all-gather.9.cloned.1.call-done, pred[]{:T(512)S(6)} %or.7), kind=kOutput, calls=%fused_computation.25 | convolution fusion | flops 1208057856 | bytes 8781825 | tf_op jit(solution)/shard_map/dot_general | solution.py:19
  143.2 6.7 %all-to-all-start = ((f32[16,8,384]{2,1,0:T(8,128)}), f32[16,8,384]{2,1,0:T(8,128)S(1)}, u32[]{:S(2)}, u32[]{:S(2)}) async-start(f32[16,8,384]{2,1,0:T(8,128)} %bitcast.42), calls=%async_computation | async-start | bytes 393216 | tf_op jit(solution)/shard_map/all_to_all | solution.py:84
  150.1 6.8 %all-to-all-done = f32[16,8,384]{2,1,0:T(8,128)S(1)} async-done(((f32[16,8,384]{2,1,0:T(8,128)}), f32[16,8,384]{2,1,0:T(8,128)S(1)}, u32[]{:S(2)}, u32[]{:S(2)}) %all-to-all-start) | async-done | bytes 196640 | tf_op jit(solution)/shard_map/all_to_all | solution.py:84
  (67 shorter events, 19.8 us)
Async XLA Ops:
  7.2 4.2 %copy-start.8 = (f32[4,24,4096]{2,1,0:T(8,128)S(1)}, f32[4,24,4096]{2,1,0:T(8,128)}, u32[]{:S(2)}) copy-start(f32[4,24,4096]{2,1,0:T(8,128)} %param.10) | copy-start | bytes 4718596
  7.2 2.3 %copy-start.11 = (s32[16]{0:T(128)S(1)}, s32[16]{0:T(128)}, u32[]{:S(2)}) copy-start(s32[16]{0:T(128)} %param.12) | copy-start | bytes 196
  7.2 88.9 %all-gather.7.cloned.1.call-start = ((), (), s32[]{:S(2)}) async-start(), calls=%async_computation.2 | async-start | bytes 13369344 | tf_op jit(solution)/shard_map/all_gather | solution.py:65
  9.4 126.7 %all-gather.9.cloned.1.call-start = ((), (), s32[]{:S(2)}) async-start(), calls=%async_computation.3 | async-start | bytes 6684672 | tf_op jit(solution)/shard_map/all_gather | solution.py:71
  11.5 11.4 %collective-permute-start.2 = (f32[24,4096]{1,0:T(8,128)S(1)}, f32[24,4096]{1,0:T(8,128)S(1)}, u32[]{:S(2)}, u32[]{:S(2)}) collective-permute-start(f32[24,4096]{1,0:T(8,128)S(1)} %get-tuple-element.42), channel_id=1, source_target_pairs={{0,8},{1,9},{2,10},{3,11},{4,12},{5,13},{6,14},{7,15},{8,0},{9,1},... | collective-permute-start | bytes 1179656 | tf_op jit(solution)/shard_map/ppermute | solution.py:56
  15.1 9.7 %collective-permute-start.3 = (f32[24,4096]{1,0:T(8,128)S(1)}, f32[24,4096]{1,0:T(8,128)S(1)}, u32[]{:S(2)}, u32[]{:S(2)}) collective-permute-start(f32[24,4096]{1,0:T(8,128)S(1)} %get-tuple-element.41), channel_id=1, source_target_pairs={{0,1},{1,0},{2,3},{3,2},{4,5},{5,4},{6,7},{7,6},{8,9},{9,8},{10,11... | collective-permute-start | bytes 1179656 | tf_op jit(solution)/shard_map/ppermute | solution.py:59
  34.0 1.9 %copy-start.10 = (s32[4]{0:T(128)S(1)}, s32[4]{0:T(128)}, u32[]{:S(2)}) copy-start(s32[4]{0:T(128)} %param.11) | copy-start | bytes 52
  40.3 47.1 %collective-permute-start = (f32[128,4096]{0,1:T(8,128)}, f32[128,4096]{0,1:T(8,128)}, u32[]{:S(2)}, u32[]{:S(2)}) collective-permute-start(f32[128,4096]{0,1:T(8,128)} %bitcast_add_fusion.3), channel_id=1, source_target_pairs={{0,8},{1,9},{2,10},{3,11},{4,12},{5,13},{6,14},{7,15},{8,0},{9,1},... | collective-permute-start | bytes 6291464 | tf_op jit(solution)/shard_map/ppermute | solution.py:57
  47.8 46.0 %collective-permute-start.1 = (f32[128,4096]{0,1:T(8,128)}, f32[128,4096]{0,1:T(8,128)}, u32[]{:S(2)}, u32[]{:S(2)}) collective-permute-start(f32[128,4096]{0,1:T(8,128)} %bitcast_add_fusion.2), channel_id=1, source_target_pairs={{0,1},{1,0},{2,3},{3,2},{4,5},{5,4},{6,7},{7,6},{8,9},{9,8},{10,11... | collective-permute-start | bytes 6291464 | tf_op jit(solution)/shard_map/ppermute | solution.py:60
  51.0 1.3 copy-start.1
  70.5 3.5 %copy-start = (f32[1,128,4096]{1,2,0:T(8,128)S(1)}, f32[1,128,4096]{1,2,0:T(8,128)}, u32[]{:S(2)}) copy-start(f32[1,128,4096]{1,2,0:T(8,128)} %copy.39) | copy-start | bytes 6291460
  70.5 3.5 %copy-start.3 = (f32[128,64,64]{0,2,1:T(8,128)S(1)}, f32[128,64,64]{0,2,1:T(8,128)}, u32[]{:S(2)}) copy-start(f32[128,64,64]{0,2,1:T(8,128)} %copy.29) | copy-start | bytes 6291460
  74.0 19.9 %copy-start.2 = (f32[1,128,4096]{1,2,0:T(8,128)S(1)}, f32[1,128,4096]{1,2,0:T(8,128)}, u32[]{:S(2)}) copy-start(f32[1,128,4096]{1,2,0:T(8,128)} %copy-done.1) | copy-start | bytes 6291460
  74.0 19.9 %copy-start.7 = (f32[128,64,64]{0,2,1:T(8,128)S(1)}, f32[128,64,64]{0,2,1:T(8,128)}, u32[]{:S(2)}) copy-start(f32[128,64,64]{0,2,1:T(8,128)} %copy.37) | copy-start | bytes 6291460
  75.5 20.6 %copy-start.4 = (f32[1,128,4096]{1,2,0:T(8,128)S(1)}, f32[1,128,4096]{1,2,0:T(8,128)}, u32[]{:S(2)}) copy-start(f32[1,128,4096]{1,2,0:T(8,128)} %bitcast_add_fusion.4) | copy-start | bytes 6291460
  96.1 9.5 %copy-start.5 = (f32[1,128,4096]{1,2,0:T(8,128)S(1)}, f32[1,128,4096]{1,2,0:T(8,128)}, u32[]{:S(2)}) copy-start(f32[1,128,4096]{1,2,0:T(8,128)} %bitcast_add_fusion.5) | copy-start | bytes 6291460
  105.7 30.4 %copy-start.6 = (f32[128,4096]{0,1:T(8,128)S(1)}, f32[128,4096]{0,1:T(8,128)}, u32[]{:S(2)}) copy-start(f32[128,4096]{0,1:T(8,128)} %fusion.11) | copy-start | bytes 6291460
  143.2 6.7 %copy-start.14 = (s32[8,2]{0,1:T(2,128)S(1)}, s32[8,2]{0,1:T(2,128)}, u32[]{:S(2)}) copy-start(s32[8,2]{0,1:T(2,128)} %param.13) | copy-start | bytes 196
  143.2 6.7 %copy-start.13 = (f32[200]{0:T(256)S(1)}, f32[200]{0:T(256)}, u32[]{:S(2)}) copy-start(f32[200]{0:T(256)} %param.14) | copy-start | bytes 2404
  143.2 13.7 %copy-start.12 = (f32[384]{0:T(512)S(1)}, f32[384]{0:T(512)}, u32[]{:S(2)}) copy-start(f32[384]{0:T(512)} %param.15) | copy-start | bytes 4612
  143.2 13.7 %all-to-all-start = ((f32[16,8,384]{2,1,0:T(8,128)}), f32[16,8,384]{2,1,0:T(8,128)S(1)}, u32[]{:S(2)}, u32[]{:S(2)}) async-start(f32[16,8,384]{2,1,0:T(8,128)} %bitcast.42), calls=%async_computation | async-start | bytes 393216 | tf_op jit(solution)/shard_map/all_to_all | solution.py:84
  156.9 0.7 copy-start.9
Sparse Core Ops, SparseCore 0:
  9.8 79.7 all-gather.6
  91.5 44.5 all-gather.8
where the time goes:
time: 165 us; the launch traced here: 164 us
  waiting for transfers between devices  48.7 us (30%)
  local copies, waits for them, and re-layouts  36.9 us (22%)
  matrix products  26.5 us (16%)
  between operations  22 us (13%)
  other arithmetic  15.4 us (9%)
  starting transfers between devices  15 us (9%)
    dot_general x3, matrix products, tile_product(): lax.dot_general(amp_tile, int_rows, (((1,), (1,)), ((), ())), precision=p...  26.5 us
    all_gather x1, waiting for transfers between devices, on_device(): lax.all_gather(third_int, 'pair', axis=0, tiled=True)  20.6 us
    ppermute x1, waiting for transfers between devices, on_device(): recv_amp = lax.ppermute(send_amp, 'virt', perm)  11.9 us
    unnamed x35, local copies, waits for them, and re-layouts  11.2 us
    mul x5, local copies, waits for them, and re-layouts, symmetric_amps(): return amp_rows + flag.astype(jnp.float32) * swap_in_tile(amp_rows)  10 us
    slice x2, local copies, waits for them, and re-layouts, own_amps(): return symmetric_amps(amplitudes[slot], tile_flags[slot])  8.97 us
    add x4, other arithmetic, symmetric_amps(): return amp_rows + flag.astype(jnp.float32) * swap_in_tile(amp_rows)  8.24 us
    all_to_all x1, waiting for transfers between devices, on_device(): received = lax.all_to_all(blocks, 'virt', 0, 0, tiled=False)  6.75 us
  transfers between devices with their start and end apart: 7, of which 6 were waited for; matrix products, arithmetic and copies ran while one was open for 41% of the time, Pallas kernels for 0%

commit v1 on v0

--- a/solution.py
+++ b/solution.py
@@ -4,6 +4,27 @@
 from jax.sharding import PartitionSpec as P
 
 TILE = 64
+
+
+def fix_widths(shard_in):
+    n_chips = lax.axis_size("pair")
+    piece_out = map(lambda w: (w, (w + 1) % n_chips), range(n_chips))
+    trail = list(piece_out)
+    so_far_all = list(map(lambda w: (w, (w - 1) % n_chips), range(n_chips)))
+    met_up, built = ([shard_in], [shard_in])
+    for _ in range(n_chips // 2):
+        met_up.append(lax.ppermute(met_up[-1], "pair", trail))
+    dd = 0
+    while dd < (n_chips - 1) // 2:
+        ready = lax.ppermute(built[-1], perm=so_far_all, axis_name="pair")
+        built.append(ready)
+        dd = dd + 1
+    placed = jnp.roll(
+        jnp.concatenate([*met_up[::-1], *built[1:]], 0),
+        shift=(lax.axis_index("pair") - n_chips // 2) * shard_in.shape[0],
+        axis=0,
+    )
+    return placed
 
 
 def swap_in_tile(rows):
@@ -68,7 +89,7 @@
     running = running + jnp.where(keep > 1, second, jnp.zeros_like(second))
     third_int = jnp.where(take > 0, recv_int, jnp.where(take_y > 0, recv_int_y, integrals[2]))
     third_amp = jnp.where(take > 0, recv_amp, jnp.where(take_y > 0, recv_amp_y, own_amps(2)))
-    third = tile_product(third_amp, lax.all_gather(third_int, "pair", axis=0, tiled=True))
+    third = tile_product(third_amp, fix_widths(third_int))
     third_live = (take > 0) | (take_y > 0) | (keep > 2)
     running = running + jnp.where(third_live, third, jnp.zeros_like(third))
 

time: 165 us -> 253 us (1.53); the launches traced: 164 us -> 249 us
  local copies, waits for them, and re-layouts: 36.9 us -> 79.7 us
  starting transfers between devices: 15 us -> 42.2 us
  waiting for transfers between devices: 48.7 us -> 64.4 us
    unnamed x35 -> x56, local copies, waits for them, and re-layouts: 11.2 us -> 53.8 us
    ppermute x1, waiting for transfers between devices: 1.1 us -> 43.3 us  [on_device(): recv_int = lax.ppermute(send_int, 'virt', perm)]
    ppermute x0 -> x15, starting transfers between devices: none -> 28.4 us  [the longest x7 21.6 us: fix_widths(): ready = lax.ppermute(built[-1], perm=so_far_all, axis_name='pair')]
    all_gather x1 -> x0, waiting for transfers between devices: 20.6 us -> none  [on_device(): lax.all_gather(third_int, 'pair', axis=0, tiled=True)]
    ppermute x0 -> x15, waiting for transfers between devices: none -> 14.5 us  [the longest x7 11.1 us: fix_widths(): ready = lax.ppermute(built[-1], perm=so_far_all, axis_name='pair')]
    ppermute x1, waiting for transfers between devices: 11.9 us -> 0.01 us  [on_device(): recv_amp = lax.ppermute(send_amp, 'virt', perm)]
    ppermute x1, waiting for transfers between devices: 6.41 us -> 0.01 us  [on_device(): lax.ppermute(symmetric_amps(amplitudes[3], tile_flags[3]), 'virt', perm_y)]
    ppermute x1, starting transfers between devices: 3.65 us -> 0.09 us  [on_device(): recv_int = lax.ppermute(send_int, 'virt', perm)]
  transfers between devices with their start and end apart: 7 -> 21, of which waited for: 6 -> 7; matrix products, arithmetic and copies ran while one was open for 41% -> 37% of each run, Pallas kernels for 0% -> 0%
where the time goes in v1:
time: 253 us; the launch traced here: 249 us
  local copies, waits for them, and re-layouts  79.7 us (32%)
  waiting for transfers between devices  64.4 us (25%)
  starting transfers between devices  42.2 us (17%)
  matrix products  26.4 us (10%)
  between operations  22.2 us (9%)
  other arithmetic  14.6 us (6%)
    unnamed x56, local copies, waits for them, and re-layouts  53.8 us
    ppermute x1, waiting for transfers between devices, on_device(): recv_int = lax.ppermute(send_int, 'virt', perm)  43.3 us
    dot_general x3, matrix products, tile_product(): lax.dot_general(amp_tile, int_rows, (((1,), (1,)), ((), ())), precision=p...  26.4 us
    ppermute x7, starting transfers between devices, fix_widths(): ready = lax.ppermute(built[-1], perm=so_far_all, axis_name='pair')  21.6 us
    ppermute x7, waiting for transfers between devices, fix_widths(): ready = lax.ppermute(built[-1], perm=so_far_all, axis_name='pair')  11.1 us
    mul x5, local copies, waits for them, and re-layouts, symmetric_amps(): return amp_rows + flag.astype(jnp.float32) * swap_in_tile(amp_rows)  8.98 us
    slice x2, local copies, waits for them, and re-layouts, own_amps(): return symmetric_amps(amplitudes[slot], tile_flags[slot])  8.77 us
    all_to_all x1, starting transfers between devices, on_device(): received = lax.all_to_all(blocks, 'virt', 0, 0, tiled=False)  7.24 us
  transfers between devices with their start and end apart: 21, of which 7 were waited for; matrix products, arithmetic and copies ran while one was open for 37% of the time, Pallas kernels for 0%

profile of v1, /device:TPU:1, one launch (start us, length us, event | category | flops | bytes accessed | tf_op | source)
XLA Modules:
  0.0 249.4 jit_solution(3620531803509570958)
XLA Ops:
  7.2 2.1 slice.66
  11.9 8.1 %fusion.33 = (f32[1,128,4096]{2,1,0:T(8,128)}, f32[1,128,4096]{2,1,0:T(8,128)}, f32[1,128,4096]{2,1,0:T(8,128)}, f32[1,128,4096]{2,1,0:T(8,128)}, f32[1,128,4096]{2,1,0:T(8,128)}) fusion(f32[4,128,4096]{2,1,0:T(8,128)} %param.9, s32[]{:T(128)S(6)} %select_n.114), kind=kLoop, calls=%fused_computation.94 | loop fusion | bytes 20971524 | tf_op jit(solution)/shard_map/slice | solution.py:84
  20.6 1.9 copy.41
  26.4 3.6 %collective-permute-start = (f32[128,4096]{0,1:T(8,128)}, f32[128,4096]{0,1:T(8,128)}, u32[]{:S(2)}, u32[]{:S(2)}) collective-permute-start(f32[128,4096]{0,1:T(8,128)} %bitcast_add_fusion.3), channel_id=1, source_target_pairs={{0,8},{1,9},{2,10},{3,11},{4,12},{5,13},{6,14},{7,15},{8,0},{9,1},... | collective-permute-start | bytes 6291464 | tf_op jit(solution)/shard_map/ppermute | solution.py:78
  33.7 1.9 copy.42
  39.6 43.3 %collective-permute-done.2 = f32[24,4096]{1,0:T(8,128)S(1)} collective-permute-done((f32[24,4096]{1,0:T(8,128)S(1)}, f32[24,4096]{1,0:T(8,128)S(1)}, u32[]{:S(2)}, u32[]{:S(2)}) %collective-permute-start.2) | collective-permute-done | bytes 393248 | tf_op jit(solution)/shard_map/ppermute | solution.py:77
  84.0 4.0 %collective-permute-start.4 = (f32[24,4096]{1,0:T(8,128)S(1)}, f32[24,4096]{1,0:T(8,128)S(1)}, u32[]{:S(2)}, u32[]{:S(2)}) collective-permute-start(f32[24,4096]{1,0:T(8,128)S(1)} %fusion.28), channel_id=1, source_target_pairs={{0,16},{16,32},{32,48},{48,64},{64,80},{80,96},{96,112},{112,128},... | collective-permute-start | bytes 1179656 | tf_op jit(solution)/shard_map/ppermute | solution.py:16
  89.4 3.4 %collective-permute-done.4 = f32[24,4096]{1,0:T(8,128)S(1)} collective-permute-done((f32[24,4096]{1,0:T(8,128)S(1)}, f32[24,4096]{1,0:T(8,128)S(1)}, u32[]{:S(2)}, u32[]{:S(2)}) %collective-permute-start.4) | collective-permute-done | bytes 393248 | tf_op jit(solution)/shard_map/ppermute | solution.py:16
  92.7 2.5 collective-permute-start.5
  103.8 4.5 %collective-permute-done.12 = f32[24,4096]{1,0:T(8,128)} collective-permute-done((f32[24,4096]{1,0:T(8,128)S(1)}, f32[24,4096]{1,0:T(8,128)}, u32[]{:S(2)}, u32[]{:S(2)}) %collective-permute-start.12) | collective-permute-done | bytes 393248 | tf_op jit(solution)/shard_map/ppermute | solution.py:19
  114.2 1.9 collective-permute-done.13
  116.1 2.8 %collective-permute-start.14 = (f32[24,4096]{1,0:T(8,128)}, f32[24,4096]{1,0:T(8,128)}, u32[]{:S(2)}, u32[]{:S(2)}) collective-permute-start(f32[24,4096]{1,0:T(8,128)} %collective-permute-done.13), channel_id=1, source_target_pairs={{0,240},{16,0},{32,16},{48,32},{64,48},{80,64},{96,80},{112,96},{1... | collective-permute-start | bytes 1179656 | tf_op jit(solution)/shard_map/ppermute | solution.py:19
  120.3 3.7 %collective-permute-done.14 = f32[24,4096]{1,0:T(8,128)} collective-permute-done((f32[24,4096]{1,0:T(8,128)}, f32[24,4096]{1,0:T(8,128)}, u32[]{:S(2)}, u32[]{:S(2)}) %collective-permute-start.14) | collective-permute-done | bytes 393248 | tf_op jit(solution)/shard_map/ppermute | solution.py:19
  123.9 3.7 %collective-permute-start.15 = (f32[24,4096]{1,0:T(8,128)}, f32[24,4096]{1,0:T(8,128)}, u32[]{:S(2)}, u32[]{:S(2)}) collective-permute-start(f32[24,4096]{1,0:T(8,128)} %collective-permute-done.14), channel_id=1, source_target_pairs={{0,240},{16,0},{32,16},{48,32},{64,48},{80,64},{96,80},{112,96},{1... | collective-permute-start | bytes 1179656 | tf_op jit(solution)/shard_map/ppermute | solution.py:19
  131.8 4.5 %collective-permute-start.16 = (f32[24,4096]{1,0:T(8,128)}, f32[24,4096]{1,0:T(8,128)}, u32[]{:S(2)}, u32[]{:S(2)}) collective-permute-start(f32[24,4096]{1,0:T(8,128)} %collective-permute-done.15), channel_id=1, source_target_pairs={{0,240},{16,0},{32,16},{48,32},{64,48},{80,64},{96,80},{112,96},{1... | collective-permute-start | bytes 1179656 | tf_op jit(solution)/shard_map/ppermute | solution.py:19
  139.1 4.1 %copy.37 = f32[128,64,64]{0,2,1:T(8,128)} copy(f32[128,64,64]{0,1,2:T(8,128)} %bitcast.97) | data formatting | bytes 4194304 | tf_op jit(solution)/shard_map/mul | solution.py:36
  144.5 3.1 %collective-permute-start.17 = (f32[24,4096]{1,0:T(8,128)}, f32[24,4096]{1,0:T(8,128)S(1)}, u32[]{:S(2)}, u32[]{:S(2)}) collective-permute-start(f32[24,4096]{1,0:T(8,128)} %collective-permute-done.16), channel_id=1, source_target_pairs={{0,240},{16,0},{32,16},{48,32},{64,48},{80,64},{96,80},{112,96},{1... | collective-permute-start | bytes 1179656 | tf_op jit(solution)/shard_map/ppermute | solution.py:19
  147.6 3.3 %fusion.13 = f32[128,4096]{0,1:T(8,128)} fusion(f32[128,4096]{0,1:T(8,128)} %collective-permute-done, f32[128,4096]{0,1:T(8,128)} %collective-permute-done.1, f32[128,64,64]{0,2,1:T(8,128)} %copy.37, f32[1,128,4096]{1,2,0:T(8,128)S(1)} %copy.43, pred[]{:T(512)} %bitcast.21, pred[]{:T(512)} %bitcast.20), kind=kLoop, calls=%fused_computation.17 | loop fusion | flops 1572864 | bytes 10485762 | tf_op jit(solution)/shard_map/jit(_where)/select_n | solution.py:91
  151.9 4.3 %collective-permute-start.18 = (f32[24,4096]{1,0:T(8,128)S(1)}, f32[24,4096]{1,0:T(8,128)S(1)}, u32[]{:S(2)}, u32[]{:S(2)}) collective-permute-start(f32[24,4096]{1,0:T(8,128)S(1)} %collective-permute-done.17), channel_id=1, source_target_pairs={{0,240},{16,0},{32,16},{48,32},{64,48},{80,64},{96,80},{112,96},{1... | collective-permute-start | bytes 1179656 | tf_op jit(solution)/shard_map/ppermute | solution.py:19
  201.2 9.5 %fusion.19 = f32[128,384]{1,0:T(8,128)S(1)} fusion(f32[2,384,4096]{2,1,0:T(8,128)} %all-gather.6.cloned.1.call-done, f32[1,128,4096]{1,2,0:T(8,128)S(1)} %copy-done, pred[]{:T(512)S(6)} %gt.29), kind=kOutput, calls=%fused_computation.25 | convolution fusion | flops 2415968256 | bytes 8585217 | tf_op jit(solution)/shard_map/dot_general | solution.py:40
  210.8 9.6 %fusion.16 = f32[128,384]{1,0:T(8,128)S(1)} fusion(f32[128,384]{1,0:T(8,128)S(1)} %fusion.19, f32[2,384,4096]{2,1,0:T(8,128)} %all-gather.6.cloned.1.call-done, f32[1,128,4096]{1,2,0:T(8,128)S(1)} %copy-done.1), kind=kOutput, calls=%fused_computation.24 | convolution fusion | flops 2415968256 | bytes 8781824 | tf_op jit(solution)/shard_map/dot_general | solution.py:40
  220.4 7.2 %fusion.25 = f32[128,384]{1,0:T(8,128)} fusion(f32[128,384]{1,0:T(8,128)S(1)} %fusion.16, f32[128,4096]{0,1:T(8,128)S(1)} %copy-done.2, f32[768,4096]{1,0:T(8,128)} %constant_dynamic-update-slice_fusion, s32[]{:T(128)S(6)} %select_n.123, pred[]{:T(512)S(6)} %or.7), kind=kOutput, calls=%fused_computation.27 | convolution fusion | flops 1208057856 | bytes 8781829 | tf_op jit(solution)/shard_map/dot_general | solution.py:40
  227.6 7.2 %all-to-all-start = ((f32[16,8,384]{2,1,0:T(8,128)}), f32[16,8,384]{2,1,0:T(8,128)S(1)}, u32[]{:S(2)}, u32[]{:S(2)}) async-start(f32[16,8,384]{2,1,0:T(8,128)} %bitcast.42), calls=%async_computation | async-start | bytes 393216 | tf_op jit(solution)/shard_map/all_to_all | solution.py:105
  235.1 6.7 %all-to-all-done = f32[16,8,384]{2,1,0:T(8,128)S(1)} async-done(((f32[16,8,384]{2,1,0:T(8,128)}), f32[16,8,384]{2,1,0:T(8,128)S(1)}, u32[]{:S(2)}, u32[]{:S(2)}) %all-to-all-start) | async-done | bytes 196640 | tf_op jit(solution)/shard_map/all_to_all | solution.py:105
  (116 shorter events, 80.4 us)
Async XLA Ops:
  7.2 194.1 %all-gather.6.cloned.1.call-start = ((), (), s32[]{:S(2)}) async-start(), calls=%async_computation.2 | async-start | bytes 13369344 | tf_op jit(solution)/shard_map/all_gather | solution.py:86
  26.4 121.3 %collective-permute-start = (f32[128,4096]{0,1:T(8,128)}, f32[128,4096]{0,1:T(8,128)}, u32[]{:S(2)}, u32[]{:S(2)}) collective-permute-start(f32[128,4096]{0,1:T(8,128)} %bitcast_add_fusion.3), channel_id=1, source_target_pairs={{0,8},{1,9},{2,10},{3,11},{4,12},{5,13},{6,14},{7,15},{8,0},{9,1},... | collective-permute-start | bytes 6291464 | tf_op jit(solution)/shard_map/ppermute | solution.py:78
  30.0 52.9 %collective-permute-start.2 = (f32[24,4096]{1,0:T(8,128)S(1)}, f32[24,4096]{1,0:T(8,128)S(1)}, u32[]{:S(2)}, u32[]{:S(2)}) collective-permute-start(f32[24,4096]{1,0:T(8,128)S(1)} %get-tuple-element.42), channel_id=1, source_target_pairs={{0,8},{1,9},{2,10},{3,11},{4,12},{5,13},{6,14},{7,15},{8,0},{9,1},... | collective-permute-start | bytes 1179656 | tf_op jit(solution)/shard_map/ppermute | solution.py:77
  30.1 52.8 %collective-permute-start.3 = (f32[24,4096]{1,0:T(8,128)S(1)}, f32[24,4096]{1,0:T(8,128)}, u32[]{:S(2)}, u32[]{:S(2)}) collective-permute-start(f32[24,4096]{1,0:T(8,128)S(1)} %get-tuple-element.41), channel_id=1, source_target_pairs={{0,1},{1,0},{2,3},{3,2},{4,5},{5,4},{6,7},{7,6},{8,9},{9,8},{10,11... | collective-permute-start | bytes 1179656 | tf_op jit(solution)/shard_map/ppermute | solution.py:80
  84.0 8.7 %collective-permute-start.4 = (f32[24,4096]{1,0:T(8,128)S(1)}, f32[24,4096]{1,0:T(8,128)S(1)}, u32[]{:S(2)}, u32[]{:S(2)}) collective-permute-start(f32[24,4096]{1,0:T(8,128)S(1)} %fusion.28), channel_id=1, source_target_pairs={{0,16},{16,32},{32,48},{48,64},{64,80},{80,96},{96,112},{112,128},... | collective-permute-start | bytes 1179656 | tf_op jit(solution)/shard_map/ppermute | solution.py:16
  92.7 9.4 %collective-permute-start.5 = (f32[24,4096]{1,0:T(8,128)S(1)}, f32[24,4096]{1,0:T(8,128)S(1)}, u32[]{:S(2)}, u32[]{:S(2)}) collective-permute-start(f32[24,4096]{1,0:T(8,128)S(1)} %collective-permute-done.4), channel_id=1, source_target_pairs={{0,16},{16,32},{32,48},{48,64},{64,80},{80,96},{96,112},{112,128},... | collective-permute-start | bytes 1179656 | tf_op jit(solution)/shard_map/ppermute | solution.py:16
  96.9 50.8 %collective-permute-start.1 = (f32[128,4096]{0,1:T(8,128)}, f32[128,4096]{0,1:T(8,128)}, u32[]{:S(2)}, u32[]{:S(2)}) collective-permute-start(f32[128,4096]{0,1:T(8,128)} %bitcast_add_fusion.2), channel_id=1, source_target_pairs={{0,1},{1,0},{2,3},{3,2},{4,5},{5,4},{6,7},{7,6},{8,9},{9,8},{10,11... | collective-permute-start | bytes 6291464 | tf_op jit(solution)/shard_map/ppermute | solution.py:81
  100.7 7.6 %collective-permute-start.12 = (f32[24,4096]{1,0:T(8,128)S(1)}, f32[24,4096]{1,0:T(8,128)}, u32[]{:S(2)}, u32[]{:S(2)}) collective-permute-start(f32[24,4096]{1,0:T(8,128)S(1)} %fusion.28), channel_id=1, source_target_pairs={{0,240},{16,0},{32,16},{48,32},{64,48},{80,64},{96,80},{112,96},{1... | collective-permute-start | bytes 1179656 | tf_op jit(solution)/shard_map/ppermute | solution.py:19
  102.1 8.0 %collective-permute-start.6 = (f32[24,4096]{1,0:T(8,128)S(1)}, f32[24,4096]{1,0:T(8,128)}, u32[]{:S(2)}, u32[]{:S(2)}) collective-permute-start(f32[24,4096]{1,0:T(8,128)S(1)} %collective-permute-done.5), channel_id=1, source_target_pairs={{0,16},{16,32},{32,48},{48,64},{64,80},{80,96},{96,112},{112,128},... | collective-permute-start | bytes 1179656 | tf_op jit(solution)/shard_map/ppermute | solution.py:16
  108.3 7.8 %collective-permute-start.13 = (f32[24,4096]{1,0:T(8,128)}, f32[24,4096]{1,0:T(8,128)}, u32[]{:S(2)}, u32[]{:S(2)}) collective-permute-start(f32[24,4096]{1,0:T(8,128)} %collective-permute-done.12), channel_id=1, source_target_pairs={{0,240},{16,0},{32,16},{48,32},{64,48},{80,64},{96,80},{112,96},{1... | collective-permute-start | bytes 1179656 | tf_op jit(solution)/shard_map/ppermute | solution.py:19
  110.1 8.8 %collective-permute-start.7 = (f32[24,4096]{1,0:T(8,128)}, f32[24,4096]{1,0:T(8,128)}, u32[]{:S(2)}, u32[]{:S(2)}) collective-permute-start(f32[24,4096]{1,0:T(8,128)} %collective-permute-done.6), channel_id=1, source_target_pairs={{0,16},{16,32},{32,48},{48,64},{64,80},{80,96},{96,112},{112,128},... | collective-permute-start | bytes 1179656 | tf_op jit(solution)/shard_map/ppermute | solution.py:16
  116.1 7.8 %collective-permute-start.14 = (f32[24,4096]{1,0:T(8,128)}, f32[24,4096]{1,0:T(8,128)}, u32[]{:S(2)}, u32[]{:S(2)}) collective-permute-start(f32[24,4096]{1,0:T(8,128)} %collective-permute-done.13), channel_id=1, source_target_pairs={{0,240},{16,0},{32,16},{48,32},{64,48},{80,64},{96,80},{112,96},{1... | collective-permute-start | bytes 1179656 | tf_op jit(solution)/shard_map/ppermute | solution.py:19
  118.9 8.7 %collective-permute-start.8 = (f32[24,4096]{1,0:T(8,128)}, f32[24,4096]{1,0:T(8,128)}, u32[]{:S(2)}, u32[]{:S(2)}) collective-permute-start(f32[24,4096]{1,0:T(8,128)} %collective-permute-done.7), channel_id=1, source_target_pairs={{0,16},{16,32},{32,48},{48,64},{64,80},{80,96},{96,112},{112,128},... | collective-permute-start | bytes 1179656 | tf_op jit(solution)/shard_map/ppermute | solution.py:16
  123.9 7.9 %collective-permute-start.15 = (f32[24,4096]{1,0:T(8,128)}, f32[24,4096]{1,0:T(8,128)}, u32[]{:S(2)}, u32[]{:S(2)}) collective-permute-start(f32[24,4096]{1,0:T(8,128)} %collective-permute-done.14), channel_id=1, source_target_pairs={{0,240},{16,0},{32,16},{48,32},{64,48},{80,64},{96,80},{112,96},{1... | collective-permute-start | bytes 1179656 | tf_op jit(solution)/shard_map/ppermute | solution.py:19
  127.6 8.7 %collective-permute-start.9 = (f32[24,4096]{1,0:T(8,128)}, f32[24,4096]{1,0:T(8,128)}, u32[]{:S(2)}, u32[]{:S(2)}) collective-permute-start(f32[24,4096]{1,0:T(8,128)} %collective-permute-done.8), channel_id=1, source_target_pairs={{0,16},{16,32},{32,48},{48,64},{64,80},{80,96},{96,112},{112,128},... | collective-permute-start | bytes 1179656 | tf_op jit(solution)/shard_map/ppermute | solution.py:16
  131.8 12.6 %collective-permute-start.16 = (f32[24,4096]{1,0:T(8,128)}, f32[24,4096]{1,0:T(8,128)}, u32[]{:S(2)}, u32[]{:S(2)}) collective-permute-start(f32[24,4096]{1,0:T(8,128)} %collective-permute-done.15), channel_id=1, source_target_pairs={{0,240},{16,0},{32,16},{48,32},{64,48},{80,64},{96,80},{112,96},{1... | collective-permute-start | bytes 1179656 | tf_op jit(solution)/shard_map/ppermute | solution.py:19
  136.4 11.3 %collective-permute-start.10 = (f32[24,4096]{1,0:T(8,128)}, f32[24,4096]{1,0:T(8,128)}, u32[]{:S(2)}, u32[]{:S(2)}) collective-permute-start(f32[24,4096]{1,0:T(8,128)} %collective-permute-done.9), channel_id=1, source_target_pairs={{0,16},{16,32},{32,48},{48,64},{64,80},{80,96},{96,112},{112,128},... | collective-permute-start | bytes 1179656 | tf_op jit(solution)/shard_map/ppermute | solution.py:16
  144.5 7.4 %collective-permute-start.17 = (f32[24,4096]{1,0:T(8,128)}, f32[24,4096]{1,0:T(8,128)S(1)}, u32[]{:S(2)}, u32[]{:S(2)}) collective-permute-start(f32[24,4096]{1,0:T(8,128)} %collective-permute-done.16), channel_id=1, source_target_pairs={{0,240},{16,0},{32,16},{48,32},{64,48},{80,64},{96,80},{112,96},{1... | collective-permute-start | bytes 1179656 | tf_op jit(solution)/shard_map/ppermute | solution.py:19
  147.6 8.6 %collective-permute-start.11 = (f32[24,4096]{1,0:T(8,128)}, f32[24,4096]{1,0:T(8,128)S(1)}, u32[]{:S(2)}, u32[]{:S(2)}) collective-permute-start(f32[24,4096]{1,0:T(8,128)} %collective-permute-done.10), channel_id=1, source_target_pairs={{0,16},{16,32},{32,48},{48,64},{64,80},{80,96},{96,112},{112,128},... | collective-permute-start | bytes 1179656 | tf_op jit(solution)/shard_map/ppermute | solution.py:16
  151.9 26.0 %collective-permute-start.18 = (f32[24,4096]{1,0:T(8,128)S(1)}, f32[24,4096]{1,0:T(8,128)S(1)}, u32[]{:S(2)}, u32[]{:S(2)}) collective-permute-start(f32[24,4096]{1,0:T(8,128)S(1)} %collective-permute-done.17), channel_id=1, source_target_pairs={{0,240},{16,0},{32,16},{48,32},{64,48},{80,64},{96,80},{112,96},{1... | collective-permute-start | bytes 1179656 | tf_op jit(solution)/shard_map/ppermute | solution.py:19
  171.7 29.5 %copy-start = (f32[1,128,4096]{1,2,0:T(8,128)S(1)}, f32[1,128,4096]{1,2,0:T(8,128)}, u32[]{:S(2)}) copy-start(f32[1,128,4096]{1,2,0:T(8,128)} %bitcast_add_fusion.4) | copy-start | bytes 6291460
  201.2 19.2 %copy-start.2 = (f32[128,4096]{0,1:T(8,128)S(1)}, f32[128,4096]{0,1:T(8,128)}, u32[]{:S(2)}) copy-start(f32[128,4096]{0,1:T(8,128)} %fusion.13) | copy-start | bytes 6291460
  227.6 14.2 %copy-start.7 = (f32[384]{0:T(512)S(1)}, f32[384]{0:T(512)}, u32[]{:S(2)}) copy-start(f32[384]{0:T(512)} %param.15) | copy-start | bytes 4612
  227.6 14.2 %all-to-all-start = ((f32[16,8,384]{2,1,0:T(8,128)}), f32[16,8,384]{2,1,0:T(8,128)S(1)}, u32[]{:S(2)}, u32[]{:S(2)}) async-start(f32[16,8,384]{2,1,0:T(8,128)} %bitcast.42), calls=%async_computation | async-start | bytes 393216 | tf_op jit(solution)/shard_map/all_to_all | solution.py:105
  (7 other events, 49.3 us)
Sparse Core Ops, SparseCore 0:
  9.8 79.7 all-gather.5
